TPU v7x, 128 devices: a whole 4x4x4 slice. The times are simulated.
128 devices in a mesh: row: 8 (over y, core), col: 16 (over z, x).
Axes of the slice: x: 4, y: 4, z: 4, core: 2. Of those that a mesh axis runs over, the one named last changes fastest.
Arguments:
- forward_head: bfloat16 [4, 2048, 1000], P(None, 'col'), may hold values from -6 to 6
- forward_tail: bfloat16 [57344, 1000], P(('col', 'row')), may hold values from -6 to 6
- forward_inverse: bfloat16 [4, 2048, 2048], P(None, 'col', 'row'), may hold values from -1.5 to 1.5, as said below
- forward_coupling: bfloat16 [6, 2048, 2048], P(None, 'row', 'col'), may hold values from -0.078125 to 0.078125
- forward_slab: bfloat16 [4, 2048, 57344], P(None, 'row', 'col'), may hold values from -0.0625 to 0.0625
- backward_head: bfloat16 [4, 2048, 1000], P(None, 'row'), may hold values from -6 to 6
- backward_tail: bfloat16 [57344, 1000], P(('row', 'col')), may hold values from -6 to 6
- backward_inverse: bfloat16 [4, 2048, 2048], P(None, 'col', 'row'), may hold values from -1.5 to 1.5, as said below
- backward_coupling: bfloat16 [6, 2048, 2048], P(None, 'row', 'col'), may hold values from -0.078125 to 0.078125
- backward_slab: bfloat16 [57344, 4, 2048], P('row', None, 'col'), may hold values from -0.0625 to 0.0625
Outputs:
- lower_head: bfloat16 [4, 2048, 1000], P(None, 'row')
- lower_tail: bfloat16 [57344, 1000], P(('col', 'row'))
- upper_head: bfloat16 [4, 2048, 1000], P(None, 'col')
- upper_tail: bfloat16 [57344, 1000], P(('row', 'col'))
Inputs may be any that keep to these rules, and one draw needn't show every extreme that they name: Each block of forward_inverse is upper triangular with diagonal entries of magnitude 0.5 to 1.5. Each block of backward_inverse is upper triangular with diagonal entries of magnitude 0.5 to 1.5.
All inputs are finite; a program needn't handle non-finite values.
Results may differ from a plain program's by a relative error of at most 0.03.
Values may be sent and summed in bfloat16 or wider, within the bound.
No kernel may reach another device: no remote copies, remote signals or barrier semaphores. Data moves between devices by JAX's collectives and lax.ppermute only.
A program may use at most 192 MiB of HBM per device.

v0:
```python
import jax
import jax.numpy as jnp
from jax import lax
from jax.sharding import PartitionSpec as P


def reduce_row(value):
    return lax.psum(value.astype(jnp.bfloat16), "row").astype(jnp.float32)


def reduce_col(value):
    return lax.psum(value.astype(jnp.bfloat16), "col").astype(jnp.float32)


def leading_dot(left, right):
    return lax.dot_general(
        left, right, (((0,), (0,)), ((), ())), preferred_element_type=jnp.float32
    )


def local(
    forward_head,
    forward_tail,
    forward_inverse,
    forward_coupling,
    forward_slab,
    backward_head,
    backward_tail,
    backward_inverse,
    backward_coupling,
    backward_slab,
):
    classes = forward_head.shape[2]
    panels = forward_head.shape[0]
    lower_list = []
    for panel_index in range(panels):
        if panel_index == 0:
            adjusted = forward_head[0]
        else:
            summed = leading_dot(
                forward_coupling[panel_index * (panel_index - 1) // 2], lower_list[0]
            )
            for earlier in range(1, panel_index):
                summed = summed + leading_dot(
                    forward_coupling[panel_index * (panel_index - 1) // 2 + earlier],
                    lower_list[earlier],
                )
            coupling = reduce_row(summed)
            adjusted = (forward_head[panel_index].astype(jnp.float32) - coupling).astype(
                jnp.bfloat16
            )
        lower_list.append(
            reduce_col(leading_dot(forward_inverse[panel_index], adjusted)).astype(jnp.bfloat16)
        )
    lower_head = jnp.stack(lower_list)
    panel_rows = lower_head.shape[1]
    flat_lower = lower_head.reshape(panels * panel_rows, classes)
    flat_slab = forward_slab.reshape(panels * panel_rows, forward_slab.shape[2])
    lower_update = lax.psum_scatter(
        leading_dot(flat_slab, flat_lower).astype(jnp.bfloat16),
        "row",
        scatter_dimension=0,
        tiled=True,
    ).astype(jnp.float32)
    lower_tail = (forward_tail.astype(jnp.float32) - lower_update).astype(jnp.bfloat16)
    upper_list = [None] * panels
    for panel_index in reversed(range(panels)):
        if panel_index == panels - 1:
            shifted = backward_head[panel_index]
        else:
            summed = None
            for later_panel in range(panel_index + 1, panels):
                block = backward_coupling[later_panel * (later_panel - 1) // 2 + panel_index]
                product = jnp.dot(
                    block, upper_list[later_panel], preferred_element_type=jnp.float32
                )
                summed = product if summed is None else summed + product
            pulled = reduce_col(summed)
            shifted = (backward_head[panel_index].astype(jnp.float32) - pulled).astype(jnp.bfloat16)
        upper_list[panel_index] = reduce_row(
            jnp.dot(backward_inverse[panel_index], shifted, preferred_element_type=jnp.float32)
        ).astype(jnp.bfloat16)
    upper_head = jnp.stack(upper_list)
    panel_cols = upper_head.shape[1]
    flat_back = backward_slab.reshape(backward_slab.shape[0], panels * panel_cols)
    flat_upper = upper_head.reshape(panels * panel_cols, classes)
    upper_update = lax.psum_scatter(
        jnp.dot(flat_back, flat_upper, preferred_element_type=jnp.float32).astype(jnp.bfloat16),
        "col",
        scatter_dimension=0,
        tiled=True,
    ).astype(jnp.float32)
    upper_tail = (backward_tail.astype(jnp.float32) - upper_update).astype(jnp.bfloat16)
    return (lower_head, lower_tail, upper_head, upper_tail)


def solution(mesh):
    in_specs = (
        P(None, "col", None),
        P(("col", "row"), None),
        P(None, "col", "row"),
        P(None, "row", "col"),
        P(None, "row", "col"),
        P(None, "row", None),
        P(("row", "col"), None),
        P(None, "col", "row"),
        P(None, "row", "col"),
        P("row", None, "col"),
    )
    out_specs = (
        P(None, "row", None),
        P(("col", "row"), None),
        P(None, "col", None),
        P(("row", "col"), None),
    )
    return jax.shard_map(local, mesh=mesh, in_specs=in_specs, out_specs=out_specs, check_vma=False)
```

profile of v0, /device:TPU:1, one launch (start us, length us, event | category | flops | bytes accessed | tf_op | source)
XLA Modules:
  0.0 793.8 jit_solution(13138176544723374713)
XLA Ops:
  7.2 2.2 convolution_convert_fusion.4
  9.5 2.1 convolution_convert_fusion.8
  11.6 87.5 %all-reduce.15.cloned.1.call-done = bf16[256,1000]{0,1:T(8,128)(2,1)} async-done(((bf16[256,1000]{0,1:T(8,128)(2,1)}), bf16[256,1000]{0,1:T(8,128)(2,1)}) %all-reduce.15.cloned.1.call-update) | async-done | bytes 512016 | tf_op jit(solution)/shard_map/psum | solution.py:12
  99.2 2.1 fusion.13
  101.3 60.2 %all-reduce.29.cloned.1.call-done = (bf16[128,1000]{0,1:T(8,128)(2,1)}, bf16[128,1000]{0,1:T(8,128)(2,1)}) async-done(((bf16[128,1000]{0,1:T(8,128)(2,1)}, bf16[128,1000]{0,1:T(8,128)(2,1)}), (bf16[128,1000]{0,1:T(8,128)(2,1)}, bf16[128,1000]{0,1:T(8,128)(2,1)})) %all-reduce.29.cloned.1.call-update) | async-done | bytes 512016 | tf_op jit(solution)/shard_map/psum | solution.py:8
  161.6 2.0 fusion.7
  163.6 2.1 fusion.10
  165.8 0.3 fusion.66
  166.0 86.8 %all-reduce.23.cloned.1.call-done = (bf16[256,1000]{0,1:T(8,128)(2,1)}, bf16[256,1000]{0,1:T(8,128)(2,1)}) async-done(((bf16[256,1000]{0,1:T(8,128)(2,1)}, bf16[256,1000]{0,1:T(8,128)(2,1)}), (bf16[256,1000]{0,1:T(8,128)(2,1)}, bf16[256,1000]{0,1:T(8,128)(2,1)})) %all-reduce.23.cloned.1.call-update) | async-done | bytes 1024016 | tf_op jit(solution)/shard_map/psum | solution.py:12
  252.8 2.2 fusion.14
  255.1 2.0 fusion.18
  257.2 59.3 %all-reduce.27.cloned.1.call-done = (bf16[128,1000]{0,1:T(8,128)(2,1)}, bf16[128,1000]{0,1:T(8,128)(2,1)}) async-done(((bf16[128,1000]{0,1:T(8,128)(2,1)}, bf16[128,1000]{0,1:T(8,128)(2,1)}), (bf16[128,1000]{0,1:T(8,128)(2,1)}, bf16[128,1000]{0,1:T(8,128)(2,1)})) %all-reduce.27.cloned.1.call-update) | async-done | bytes 512016 | tf_op jit(solution)/shard_map/psum | solution.py:8
  316.5 1.3 fusion.54
  317.8 1.1 fusion.6
  318.9 1.1 fusion.8
  320.1 0.3 fusion.62
  320.4 0.3 convolution_add_fusion.4
  320.7 87.0 %all-reduce.21.cloned.1.call-done = (bf16[256,1000]{0,1:T(8,128)(2,1)}, bf16[256,1000]{0,1:T(8,128)(2,1)}) async-done(((bf16[256,1000]{0,1:T(8,128)(2,1)}, bf16[256,1000]{0,1:T(8,128)(2,1)}), (bf16[256,1000]{0,1:T(8,128)(2,1)}, bf16[256,1000]{0,1:T(8,128)(2,1)})) %all-reduce.21.cloned.1.call-update) | async-done | bytes 1024016 | tf_op jit(solution)/shard_map/psum | solution.py:12
  407.7 2.2 fusion.15
  409.9 2.0 fusion.17
  412.0 59.3 %all-reduce.25.cloned.1.call-done = (bf16[128,1000]{0,1:T(8,128)(2,1)}, bf16[128,1000]{0,1:T(8,128)(2,1)}) async-done(((bf16[128,1000]{0,1:T(8,128)(2,1)}, bf16[128,1000]{0,1:T(8,128)(2,1)}), (bf16[128,1000]{0,1:T(8,128)(2,1)}, bf16[128,1000]{0,1:T(8,128)(2,1)})) %all-reduce.25.cloned.1.call-update) | async-done | bytes 512016 | tf_op jit(solution)/shard_map/psum | solution.py:8
  471.3 1.3 fusion.50
  472.6 1.2 convolution_add_fusion.1
  473.8 2.0 fusion.5
  475.8 2.0 fusion.9
  477.8 87.1 %all-reduce.19.cloned.1.call-done = (bf16[1,256,1000]{1,2,0:T(8,128)(2,1)}, bf16[256,1000]{0,1:T(8,128)(2,1)}) async-done(((bf16[1,256,1000]{1,2,0:T(8,128)(2,1)}, bf16[256,1000]{0,1:T(8,128)(2,1)}), (bf16[1,256,1000]{1,2,0:T(8,128)(2,1)}, bf16[256,1000]{0,1:T(8,128)(2,1)})) %all-reduce.19.cloned.1.call-update) | async-done | bytes 1024016 | tf_op jit(solution)/shard_map/psum | solution.py:12
  565.0 2.2 fusion.16
  567.2 1.3 pad_maximum_fusion
  568.6 1.3 copy-done.4
  569.8 12.5 %fusion.2 = bf16[3584,1000]{0,1:T(8,128)(2,1)} fusion(bf16[4,256,1000]{1,2,0:T(8,128)(2,1)S(1)} %pad_maximum_fusion, bf16[4,256,3584]{2,1,0:T(8,128)(2,1)} %param.14), kind=kOutput, calls=%fused_computation.4 | convolution fusion | flops 7343616000 | bytes 16556032 | tf_op jit(solution)/shard_map/dot_general | solution.py:16
  582.4 10.3 %copy.24 = bf16[3584,1000]{1,0:T(8,128)(2,1)} copy(bf16[3584,1000]{0,1:T(8,128)(2,1)} %fusion.2) | data formatting | bytes 14336000
  593.0 33.0 %all-reduce.17.cloned.1.call-done = bf16[1,128,1000]{1,2,0:T(8,128)(2,1)} async-done(((bf16[1,128,1000]{1,2,0:T(8,128)(2,1)}), bf16[1,128,1000]{1,2,0:T(8,128)(2,1)}) %all-reduce.17.cloned.1.call-update) | async-done | bytes 256016 | tf_op jit(solution)/shard_map/psum | solution.py:8
  626.0 1.1 pad_maximum_fusion.1
  627.1 0.9 copy-done.6
  628.1 13.4 %fusion = bf16[7168,1000]{0,1:T(8,128)(2,1)} fusion(bf16[4,128,1000]{1,2,0:T(8,128)(2,1)S(1)} %pad_maximum_fusion.1, bf16[7168,4,128]{2,1,0:T(4,128)(2,1)} %param.19), kind=kOutput, calls=%fused_computation.2 | convolution fusion | flops 7347200000 | bytes 22700032 | tf_op jit(solution)/shard_map/dot_general | solution.py:88
  641.5 20.0 %copy.26 = bf16[7168,1000]{1,0:T(8,128)(2,1)} copy(bf16[7168,1000]{0,1:T(8,128)(2,1)} %fusion) | data formatting | bytes 28672000
  661.5 1.2 copy-done.9
  662.7 0.7 copy.20
  663.5 0.5 copy-done.10
  663.9 0.7 copy.19
  664.7 12.0 %reduce-scatter.7.cloned.1.call-done = bf16[448,1000]{1,0:T(8,128)(2,1)} async-done(((bf16[3584,1000]{1,0:T(8,128)(2,1)}), bf16[448,1000]{1,0:T(8,128)(2,1)}) %reduce-scatter.7.cloned.1.call-update) | async-done | bytes 896016
  676.7 2.2 copy.25
  678.9 2.6 subtract_convert_fusion.1
  681.5 2.2 copy.22
  683.7 98.0 %reduce-scatter.9.cloned.1.call-done = bf16[448,1000]{1,0:T(8,128)(2,1)} async-done(((bf16[7168,1000]{1,0:T(8,128)(2,1)}), bf16[448,1000]{1,0:T(8,128)(2,1)}) %reduce-scatter.9.cloned.1.call-update) | async-done | bytes 896016
  781.8 1.7 copy.27
  783.4 1.3 subtract_convert_fusion
  784.8 2.2 copy.23
  (48 shorter events, 0.8 us)
Async XLA Ops:
  7.2 154.4 %copy-start.8 = (bf16[4,128,1000]{1,2,0:T(8,128)(2,1)S(1)}, bf16[4,128,1000]{1,2,0:T(8,128)(2,1)}, u32[]{:S(2)}) copy-start(bf16[4,128,1000]{1,2,0:T(8,128)(2,1)} %param.10) | copy-start | bytes 3072004
  7.2 154.4 %copy-start.13 = (bf16[4,128,256]{2,1,0:T(8,128)(2,1)S(1)}, bf16[4,128,256]{2,1,0:T(8,128)(2,1)}, u32[]{:S(2)}) copy-start(bf16[4,128,256]{2,1,0:T(8,128)(2,1)} %param.12) | copy-start | bytes 786436
  7.2 92.0 %copy-start.11 = (bf16[6,256,128]{2,1,0:T(8,128)(2,1)S(1)}, bf16[6,256,128]{2,1,0:T(8,128)(2,1)}, u32[]{:S(2)}) copy-start(bf16[6,256,128]{2,1,0:T(8,128)(2,1)} %param.13) | copy-start | bytes 1179652
  7.2 92.0 %all-reduce.15.cloned.1.call-start = ((), (), s32[]{:S(2)}) async-start(), calls=%async_computation.2 | async-start | bytes 1024000 | tf_op jit(solution)/shard_map/psum | solution.py:12
  9.4 154.2 %copy-start.12 = (bf16[6,256,128]{2,1,0:T(8,128)(2,1)S(1)}, bf16[6,256,128]{2,1,0:T(8,128)(2,1)}, u32[]{:S(2)}) copy-start(bf16[6,256,128]{2,1,0:T(8,128)(2,1)} %param.18) | copy-start | bytes 1179652
  9.4 152.1 %all-reduce.29.cloned.1.call-start = ((), (), s32[]{:S(2)}) async-start(), calls=%async_computation.11 | async-start | bytes 1024000 | tf_op jit(solution)/shard_map/psum | solution.py:8
  99.2 66.6 %copy-start = (bf16[256,1000]{0,1:T(8,128)(2,1)S(1)}, bf16[256,1000]{0,1:T(8,128)(2,1)}, u32[]{:S(2)}) copy-start(bf16[256,1000]{0,1:T(8,128)(2,1)} %all-reduce.15.cloned.1.call-done) | copy-start | bytes 1536004
  101.3 151.6 %all-reduce.23.cloned.1.call-start = ((), (), s32[]{:S(2)}) async-start(), calls=%async_computation.8 | async-start | bytes 2048000 | tf_op jit(solution)/shard_map/psum | solution.py:12
  165.7 150.8 %all-reduce.27.cloned.1.call-start = ((), (), s32[]{:S(2)}) async-start(), calls=%async_computation.10 | async-start | bytes 1024000 | tf_op jit(solution)/shard_map/psum | solution.py:8
  252.8 65.0 %copy-start.2 = (bf16[128,1000]{0,1:T(8,128)(2,1)S(1)}, bf16[128,1000]{0,1:T(8,128)(2,1)}, u32[]{:S(2)}) copy-start(bf16[128,1000]{0,1:T(8,128)(2,1)} %get-tuple-element.23) | copy-start | bytes 768004
  257.1 150.5 %all-reduce.21.cloned.1.call-start = ((), (), s32[]{:S(2)}) async-start(), calls=%async_computation.7 | async-start | bytes 2048000 | tf_op jit(solution)/shard_map/psum | solution.py:12
  316.5 2.5 copy-start.15
  318.9 1.4 copy-start.1
  320.0 151.3 %all-reduce.25.cloned.1.call-start = ((), (), s32[]{:S(2)}) async-start(), calls=%async_computation.9 | async-start | bytes 1024000 | tf_op jit(solution)/shard_map/psum | solution.py:8
  407.7 64.9 %copy-start.3 = (bf16[128,1000]{0,1:T(8,128)(2,1)S(1)}, bf16[128,1000]{0,1:T(8,128)(2,1)}, u32[]{:S(2)}) copy-start(bf16[128,1000]{0,1:T(8,128)(2,1)} %get-tuple-element.21) | copy-start | bytes 768004
  412.0 153.0 %all-reduce.19.cloned.1.call-start = ((), (), s32[]{:S(2)}) async-start(), calls=%async_computation.6 | async-start | bytes 2048000 | tf_op jit(solution)/shard_map/psum | solution.py:12
  472.6 3.2 copy-start.14
  475.8 91.5 %copy-start.5 = (bf16[256,1000]{0,1:T(8,128)(2,1)S(1)}, bf16[256,1000]{0,1:T(8,128)(2,1)}, u32[]{:S(2)}) copy-start(bf16[256,1000]{0,1:T(8,128)(2,1)} %get-tuple-element.14) | copy-start | bytes 1536004
  477.8 148.2 %all-reduce.17.cloned.1.call-start = ((), (), s32[]{:S(2)}) async-start(), calls=%async_computation.3 | async-start | bytes 512000 | tf_op jit(solution)/shard_map/psum | solution.py:8
  567.2 109.5 %reduce-scatter.7.cloned.1.call-start = ((), (), s32[]{:S(2)}) async-start(), calls=%async_computation.4 | async-start | bytes 8257536
  568.5 1.3 copy-start.4
  592.7 33.3 %copy-start.7 = (bf16[128,1000]{0,1:T(8,128)(2,1)S(1)}, bf16[128,1000]{0,1:T(8,128)(2,1)}, u32[]{:S(2)}) copy-start(bf16[128,1000]{0,1:T(8,128)(2,1)} %get-tuple-element.19) | copy-start | bytes 768004
  592.8 189.0 %reduce-scatter.9.cloned.1.call-start = ((), (), s32[]{:S(2)}) async-start(), calls=%async_computation.5 | async-start | bytes 15597568
  627.1 1.0 copy-start.6
  661.5 1.2 copy-start.9
  662.7 1.2 copy-start.10
Sparse Core Ops, SparseCore 0:
  11.8 87.2 all-reduce.14
  102.4 59.1 all-reduce.28
  165.8 86.9 all-reduce.22
  257.3 59.1 all-reduce.26
  320.6 86.9 all-reduce.20
  412.1 59.1 all-reduce.24
  477.9 86.9 all-reduce.18
  567.9 58.1 all-reduce.16
  628.6 48.0 reduce-scatter.6
  680.3 101.3 reduce-scatter.8
where the time goes:
time: 795 us; the launch traced here: 794 us
  waiting for transfers between devices  670 us (84%)
  matrix products  58 us (7%)
  local copies, waits for them, and re-layouts  44.1 us (6%)
  between operations  14.3 us (2%)
    psum x4, waiting for transfers between devices, reduce_col(): return lax.psum(value.astype(jnp.bfloat16), 'col').astype(jnp.float32)  348 us
    psum x4, waiting for transfers between devices, reduce_row(): return lax.psum(value.astype(jnp.bfloat16), 'row').astype(jnp.float32)  212 us
    unnamed x12, waiting for transfers between devices  110 us
    unnamed x40, local copies, waits for them, and re-layouts  44.1 us
    dot_general x11, matrix products, leading_dot(): lax.dot_general(left, right, (((0,), (0,)), ((), ())), preferred_element_...  26.8 us
  transfers between devices with their start and end apart: 10, of which 10 were waited for; matrix products, arithmetic and copies ran while one was open for 9% of the time, Pallas kernels for 0%

commit v1 on v0

--- a/solution.py
+++ b/solution.py
@@ -9,7 +9,7 @@
 
 
 def reduce_col(value):
-    return lax.psum(value.astype(jnp.bfloat16), "col").astype(jnp.float32)
+    return jnp.sum(lax.all_gather(value.astype(jnp.bfloat16), "col"), axis=0).astype(jnp.float32)
 
 
 def leading_dot(left, right):

time: 795 us -> 964 us (1.21); the launches traced: 794 us -> 953 us
  waiting for transfers between devices: 670 us -> 747 us
  local copies, waits for them, and re-layouts: 44.1 us -> 87.7 us
  other arithmetic: 6.27 us -> 37.6 us
    all_gather x0 -> x7, waiting for transfers between devices: none -> 398 us  [reduce_col(): lax.all_gather(value.astype(jnp.bfloat16), 'col')]
    psum x4 -> x0, waiting for transfers between devices: 348 us -> none  [reduce_col(): return lax.psum(value.astype(jnp.bfloat16), 'col').astype(jnp.float32)]
    unnamed x40 -> x45, local copies, waits for them, and re-layouts: 44.1 us -> 87.7 us
    reduce_sum x0 -> x7, other arithmetic: none -> 34.4 us  [reduce_col(): jnp.sum(lax.all_gather(value.astype(jnp.bfloat16), 'col'), axis=0)]
    psum x4, waiting for transfers between devices: 212 us -> 238 us  [reduce_row(): return lax.psum(value.astype(jnp.bfloat16), 'row').astype(jnp.float32)]
    unnamed x12 -> x15, waiting for transfers between devices: 110 us -> 110 us
  transfers between devices with their start and end apart: 10 -> 13, of which waited for: 10 -> 13; matrix products, arithmetic and copies ran while one was open for 9% -> 14% of each run, Pallas kernels for 0% -> 0%
where the time goes in v1:
time: 964 us; the launch traced here: 953 us
  waiting for transfers between devices  747 us (77%)
  local copies, waits for them, and re-layouts  87.7 us (9%)
  matrix products  64 us (7%)
  other arithmetic  37.6 us (4%)
  between operations  16 us (2%)
    all_gather x7, waiting for transfers between devices, reduce_col(): lax.all_gather(value.astype(jnp.bfloat16), 'col')  398 us
    psum x4, waiting for transfers between devices, reduce_row(): return lax.psum(value.astype(jnp.bfloat16), 'row').astype(jnp.float32)  238 us
    unnamed x15, waiting for transfers between devices  110 us
    unnamed x45, local copies, waits for them, and re-layouts  87.7 us
    reduce_sum x7, other arithmetic, reduce_col(): jnp.sum(lax.all_gather(value.astype(jnp.bfloat16), 'col'), axis=0)  34.4 us
    dot_general x11, matrix products, leading_dot(): lax.dot_general(left, right, (((0,), (0,)), ((), ())), preferred_element_...  32 us
  transfers between devices with their start and end apart: 13, of which 13 were waited for; matrix products, arithmetic and copies ran while one was open for 14% of the time, Pallas kernels for 0%

profile of v1, /device:TPU:1, one launch (start us, length us, event | category | flops | bytes accessed | tf_op | source)
XLA Modules:
  0.0 952.9 jit_solution(1053346349753376828)
XLA Ops:
  8.0 2.1 convolution_convert_fusion.8
  10.2 2.1 convolution_convert_fusion.4
  12.3 61.1 %all-reduce.8.cloned.1.call-done = bf16[128,1000]{0,1:T(8,128)(2,1)} async-done(((bf16[128,1000]{0,1:T(8,128)(2,1)}), bf16[128,1000]{0,1:T(8,128)(2,1)}) %all-reduce.8.cloned.1.call-update) | async-done | bytes 256016 | tf_op jit(solution)/shard_map/psum | solution.py:8
  73.4 2.1 fusion.10
  75.6 16.5 %all-gather.15.cloned.1.call-done = bf16[4096,1000]{0,1:T(8,128)(2,1)} async-done(((bf16[256,1000]{0,1:T(8,128)(2,1)}), bf16[4096,1000]{0,1:T(8,128)(2,1)}) %all-gather.15.cloned.1.call-update) | async-done | bytes 8192016 | tf_op jit(solution)/shard_map/all_gather | solution.py:12
  92.1 6.4 copy.28
  98.5 4.7 bitcast_reduce_fusion.6
  104.0 1.8 fusion.13
  105.8 65.1 %all-gather.23.cloned.1.call-done = bf16[4096,1000]{0,1:T(8,128)(2,1)} async-done(((bf16[256,1000]{0,1:T(8,128)(2,1)}), bf16[4096,1000]{0,1:T(8,128)(2,1)}) %all-gather.23.cloned.1.call-update) | async-done | bytes 8192016 | tf_op jit(solution)/shard_map/all_gather | solution.py:12
  170.9 6.4 copy.32
  177.3 5.1 bitcast_reduce_fusion.2
  182.4 2.1 fusion.14
  184.6 59.1 %all-reduce.14.cloned.1.call-done = (bf16[128,1000]{0,1:T(8,128)(2,1)}, bf16[128,1000]{0,1:T(8,128)(2,1)}) async-done(((bf16[128,1000]{0,1:T(8,128)(2,1)}, bf16[128,1000]{0,1:T(8,128)(2,1)}), (bf16[128,1000]{0,1:T(8,128)(2,1)}, bf16[128,1000]{0,1:T(8,128)(2,1)})) %all-reduce.14.cloned.1.call-update) | async-done | bytes 512016 | tf_op jit(solution)/shard_map/psum | solution.py:8
  243.7 2.2 fusion.7
  247.2 2.1 fusion.6
  249.4 1.9 fusion.69
  251.3 71.4 %all-gather.17.cloned.1.call-done = bf16[4096,1000]{0,1:T(8,128)(2,1)} async-done(((bf16[256,1000]{0,1:T(8,128)(2,1)}), bf16[4096,1000]{0,1:T(8,128)(2,1)}) %all-gather.17.cloned.1.call-update) | async-done | bytes 8192016 | tf_op jit(solution)/shard_map/all_gather | solution.py:12
  322.8 6.4 copy.29
  329.1 5.5 bitcast_reduce_fusion.5
  334.6 66.9 %all-gather.25.cloned.1.call-done = bf16[4096,1000]{0,1:T(8,128)(2,1)} async-done(((bf16[256,1000]{0,1:T(8,128)(2,1)}), bf16[4096,1000]{0,1:T(8,128)(2,1)}) %all-gather.25.cloned.1.call-update) | async-done | bytes 8192016 | tf_op jit(solution)/shard_map/all_gather | solution.py:12
  401.5 6.4 copy.33
  407.8 4.9 bitcast_reduce_fusion.1
  412.7 2.1 fusion.15
  414.9 1.8 fusion.18
  416.8 59.1 %all-reduce.12.cloned.1.call-done = (bf16[128,1000]{0,1:T(8,128)(2,1)}, bf16[128,1000]{0,1:T(8,128)(2,1)}) async-done(((bf16[128,1000]{0,1:T(8,128)(2,1)}, bf16[128,1000]{0,1:T(8,128)(2,1)}), (bf16[128,1000]{0,1:T(8,128)(2,1)}, bf16[128,1000]{0,1:T(8,128)(2,1)})) %all-reduce.12.cloned.1.call-update) | async-done | bytes 512016 | tf_op jit(solution)/shard_map/psum | solution.py:8
  478.5 2.1 fusion.5
  480.7 2.2 fusion.8
  484.1 1.9 convolution_add_fusion.4
  486.0 71.5 %all-gather.27.cloned.1.call-done = bf16[4096,1000]{0,1:T(8,128)(2,1)} async-done(((bf16[256,1000]{0,1:T(8,128)(2,1)}), bf16[4096,1000]{0,1:T(8,128)(2,1)}) %all-gather.27.cloned.1.call-update) | async-done | bytes 8192016 | tf_op jit(solution)/shard_map/all_gather | solution.py:12
  557.5 6.4 copy.34
  563.9 4.7 bitcast_reduce_fusion
  568.5 2.0 fusion.16
  570.6 65.8 %all-gather.19.cloned.1.call-done = bf16[4096,1000]{0,1:T(8,128)(2,1)} async-done(((bf16[256,1000]{0,1:T(8,128)(2,1)}), bf16[4096,1000]{0,1:T(8,128)(2,1)}) %all-gather.19.cloned.1.call-update) | async-done | bytes 8192016 | tf_op jit(solution)/shard_map/all_gather | solution.py:12
  636.4 6.4 copy.30
  642.8 4.9 bitcast_reduce_fusion.4
  648.5 1.8 fusion.17
  650.4 59.1 %all-reduce.10.cloned.1.call-done = (bf16[128,1000]{0,1:T(8,128)(2,1)}, bf16[1,128,1000]{1,2,0:T(8,128)(2,1)}) async-done(((bf16[128,1000]{0,1:T(8,128)(2,1)}, bf16[1,128,1000]{1,2,0:T(8,128)(2,1)}), (bf16[128,1000]{0,1:T(8,128)(2,1)}, bf16[1,128,1000]{1,2,0:T(8,128)(2,1)})) %all-reduce.10.cloned.1.call-update) | async-done | bytes 512016 | tf_op jit(solution)/shard_map/psum | solution.py:8
  709.5 2.2 fusion.9
  714.1 13.5 %fusion = bf16[7168,1000]{0,1:T(8,128)(2,1)} fusion(bf16[4,128,1000]{1,2,0:T(8,128)(2,1)S(1)} %pad_maximum_fusion.1, bf16[7168,4,128]{2,1,0:T(4,128)(2,1)} %param.19), kind=kOutput, calls=%fused_computation.2 | convolution fusion | flops 7347200000 | bytes 22700032 | tf_op jit(solution)/shard_map/dot_general | solution.py:88
  727.7 19.8 %copy.26 = bf16[7168,1000]{1,0:T(8,128)(2,1)} copy(bf16[7168,1000]{0,1:T(8,128)(2,1)} %fusion) | data formatting | bytes 28672000
  748.0 40.5 %all-gather.21.cloned.1.call-done = bf16[4096,1000]{0,1:T(8,128)(2,1)} async-done(((bf16[256,1000]{0,1:T(8,128)(2,1)}), bf16[4096,1000]{0,1:T(8,128)(2,1)}) %all-gather.21.cloned.1.call-update) | async-done | bytes 8192016 | tf_op jit(solution)/shard_map/all_gather | solution.py:12
  788.5 6.4 copy.31
  794.9 4.7 bitcast_reduce_fusion.3
  801.2 12.9 %fusion.2 = bf16[3584,1000]{0,1:T(8,128)(2,1)} fusion(bf16[4,256,1000]{1,2,0:T(8,128)(2,1)S(1)} %pad_maximum_fusion, bf16[4,256,3584]{2,1,0:T(8,128)(2,1)} %param.14), kind=kOutput, calls=%fused_computation.11 | convolution fusion | flops 7343616000 | bytes 16556032 | tf_op jit(solution)/shard_map/dot_general | solution.py:16
  814.2 10.6 %copy.24 = bf16[3584,1000]{1,0:T(8,128)(2,1)} copy(bf16[3584,1000]{0,1:T(8,128)(2,1)} %fusion.2) | data formatting | bytes 14336000
  826.7 66.9 %reduce-scatter.9.cloned.1.call-done = bf16[448,1000]{1,0:T(8,128)(2,1)} async-done(((bf16[7168,1000]{1,0:T(8,128)(2,1)}), bf16[448,1000]{1,0:T(8,128)(2,1)}) %reduce-scatter.9.cloned.1.call-update) | async-done | bytes 896016
  896.6 2.2 copy.23
  898.8 43.1 %reduce-scatter.7.cloned.1.call-done = bf16[448,1000]{1,0:T(8,128)(2,1)} async-done(((bf16[3584,1000]{1,0:T(8,128)(2,1)}), bf16[448,1000]{1,0:T(8,128)(2,1)}) %reduce-scatter.7.cloned.1.call-update) | async-done | bytes 896016
  (69 shorter events, 20.0 us)
Async XLA Ops:
  8.0 65.5 %all-reduce.8.cloned.1.call-start = ((), (), s32[]{:S(2)}) async-start(), calls=%async_computation.2 | async-start | bytes 512000 | tf_op jit(solution)/shard_map/psum | solution.py:8
  10.1 82.0 %all-gather.15.cloned.1.call-start = ((), (), s32[]{:S(2)}) async-start(), calls=%async_computation.3 | async-start | bytes 8704000 | tf_op jit(solution)/shard_map/all_gather | solution.py:12
  12.3 158.6 %all-gather.23.cloned.1.call-start = ((), (), s32[]{:S(2)}) async-start(), calls=%async_computation.7 | async-start | bytes 8704000 | tf_op jit(solution)/shard_map/all_gather | solution.py:12
  75.6 168.1 %all-reduce.14.cloned.1.call-start = ((), (), s32[]{:S(2)}) async-start(), calls=%async_computation.14 | async-start | bytes 1024000 | tf_op jit(solution)/shard_map/psum | solution.py:8
  103.2 0.8 copy-start
  182.4 67.0 %copy-start.1 = (bf16[256,1000]{0,1:T(8,128)(2,1)S(1)}, bf16[256,1000]{0,1:T(8,128)(2,1)}, u32[]{:S(2)}) copy-start(bf16[256,1000]{0,1:T(8,128)(2,1)} %copy-done) | copy-start | bytes 1536004
  184.5 138.2 %all-gather.17.cloned.1.call-start = ((), (), s32[]{:S(2)}) async-start(), calls=%async_computation.4 | async-start | bytes 8704000 | tf_op jit(solution)/shard_map/all_gather | solution.py:12
  245.9 155.6 %all-gather.25.cloned.1.call-start = ((), (), s32[]{:S(2)}) async-start(), calls=%async_computation.8 | async-start | bytes 8704000 | tf_op jit(solution)/shard_map/all_gather | solution.py:12
  249.3 226.6 %all-reduce.12.cloned.1.call-start = ((), (), s32[]{:S(2)}) async-start(), calls=%async_computation.13 | async-start | bytes 1024000 | tf_op jit(solution)/shard_map/psum | solution.py:8
  407.8 7.0 copy-start.4
  407.8 7.0 copy-start.11
  412.7 70.2 %copy-start.2 = (bf16[256,1000]{0,1:T(8,128)(2,1)S(1)}, bf16[256,1000]{0,1:T(8,128)(2,1)}, u32[]{:S(2)}) copy-start(bf16[256,1000]{0,1:T(8,128)(2,1)} %copy-done) | copy-start | bytes 1536004
  412.7 71.3 %copy-start.5 = (bf16[256,1000]{0,1:T(8,128)(2,1)S(1)}, bf16[256,1000]{0,1:T(8,128)(2,1)}, u32[]{:S(2)}) copy-start(bf16[256,1000]{0,1:T(8,128)(2,1)} %bitcast_reduce_fusion.5) | copy-start | bytes 1536004
  416.7 140.8 %all-gather.27.cloned.1.call-start = ((), (), s32[]{:S(2)}) async-start(), calls=%async_computation.9 | async-start | bytes 8704000 | tf_op jit(solution)/shard_map/all_gather | solution.py:12
  480.6 155.8 %all-gather.19.cloned.1.call-start = ((), (), s32[]{:S(2)}) async-start(), calls=%async_computation.5 | async-start | bytes 8704000 | tf_op jit(solution)/shard_map/all_gather | solution.py:12
  482.9 226.6 %all-reduce.10.cloned.1.call-start = ((), (), s32[]{:S(2)}) async-start(), calls=%async_computation.12 | async-start | bytes 1024000 | tf_op jit(solution)/shard_map/psum | solution.py:8
  642.8 5.7 copy-start.10
  647.7 0.8 copy-start.7
  650.3 138.2 %all-gather.21.cloned.1.call-start = ((), (), s32[]{:S(2)}) async-start(), calls=%async_computation.6 | async-start | bytes 8704000 | tf_op jit(solution)/shard_map/all_gather | solution.py:12
  711.7 182.0 %reduce-scatter.9.cloned.1.call-start = ((), (), s32[]{:S(2)}) async-start(), calls=%async_computation.11 | async-start | bytes 15597568
  713.2 1.0 copy-start.12
  747.5 194.4 %reduce-scatter.7.cloned.1.call-start = ((), (), s32[]{:S(2)}) async-start(), calls=%async_computation.10 | async-start | bytes 8257536
  794.9 4.7 copy-start.3
  794.9 4.7 copy-start.6
  794.9 4.7 copy-start.8
  799.9 1.3 copy-start.9
  814.2 10.6 %copy-start.13 = (bf16[448,1000]{1,0:T(8,128)(2,1)S(1)}, bf16[448,1000]{1,0:T(8,128)(2,1)}, u32[]{:S(2)}) copy-start(bf16[448,1000]{1,0:T(8,128)(2,1)} %param.16) | copy-start | bytes 2688004
  824.8 1.2 copy-start.14
Sparse Core Ops, SparseCore 0:
  11.7 61.6 all-reduce.7
  184.7 58.9 all-reduce.13
  416.9 59.0 all-reduce.11
  650.4 58.9 all-reduce.9
Sparse Core Ops, SparseCore 1:
  13.3 78.8 all-gather.14
  94.9 75.9 all-gather.22
  246.0 76.7 all-gather.16
  325.5 75.9 all-gather.24
  480.7 76.7 all-gather.26
  560.4 75.9 all-gather.18
  711.7 76.7 all-gather.20
  791.8 101.8 reduce-scatter.8
  895.9 46.0 reduce-scatter.6
